TPU v7x, 32 devices: a whole 2x2x4 slice. The times are simulated.
32 devices in a mesh: pulse: 16 (over z, x, core), range: 2 (over y).
Axes of the slice: x: 2, y: 2, z: 4, core: 2. Of those that a mesh axis runs over, the one named last changes fastest.
Arguments:
- echo: bfloat16 [32, 2, 32768], P('pulse', None, 'range'), may hold values from -6 to 6
- chirp_phase: float32 [256], replicated, may hold values from -0.5 to 201.5624
- rec_phase: float32 [2, 2048, 2], P('range', 'pulse'), may hold values from -3.140625 to 3.140625
- rec_start: int32 [2, 2048], P('range', 'pulse'), may hold values from 0 to 32256
- rec_owner: int32 [2, 2048, 1], P('range', 'pulse'), may hold values from 0 to 31; in each aligned block of 128 rows (0 to 127, 128 to 255, ..., all dimensions but the last counted through in order) at most 6 rows name the same one
- rec_row: int32 [2, 2048], P('range', 'pulse'), may hold values from 0 to 63
- rec_weight: float32 [2, 2048], P('range', 'pulse'), may hold values from 0.2 to 1
- rec_count: int32 [2, 16], P('range', 'pulse'), may hold values from 96 to 128, as said below
- prior: bfloat16 [512, 2, 1024], P('pulse', None, 'range'), may hold values from -6 to 6
- interp_weight: bfloat16 [64, 32], replicated, may hold values from -1 to 1
Outputs:
- tiles: float32 [1024, 2, 1024], P('pulse', None, 'range')
Inputs may be any that keep to these rules, and one draw needn't show every extreme that they name: `rec_owner`: in each aligned block of 128 record slots (one device's slots) no owner is named more than 6 times. Owner o is the tile of pulse index o // 2 and range index o % 2, 2 being the number of range devices. `rec_count`: some subimage has all 128 slots live.
All inputs are finite; a program needn't handle non-finite values.
Results may differ from a plain program's by a relative error of at most 0.0034.
Values may be sent and summed in bfloat16 or wider, within the bound.
No kernel may reach another device: no remote copies, remote signals or barrier semaphores. Data moves between devices by JAX's collectives and lax.ppermute only.
A program may use at most 64 MiB of HBM per device.

v0:
```python
import jax
import jax.numpy as jnp
from jax import lax
from jax.sharding import PartitionSpec as P

SEG = 512


def chirp_matrix(chirp_phase):
    tap_count = chirp_phase.shape[0]
    tap_scale = 1.0 / jnp.sqrt(jnp.float32(tap_count))
    real_taps = jnp.cos(chirp_phase) * tap_scale
    imag_taps = jnp.sin(chirp_phase) * tap_scale

    def banded(values):
        padded = jnp.concatenate([values, jnp.zeros((tap_count + 1,), jnp.float32)])
        return (
            jnp.tile(padded, tap_count)[: 2 * tap_count * tap_count]
            .reshape(tap_count, 2 * tap_count)
            .T
        )

    real_band = banded(real_taps)
    imag_band = banded(imag_taps)
    upper = jnp.concatenate([real_band, -imag_band], axis=1)
    lower = jnp.concatenate([imag_band, real_band], axis=1)
    return jnp.concatenate([upper, lower], axis=0).astype(jnp.bfloat16)


def compress(echo_block, tail_rim, filter_matrix):
    pulses, planes, bin_count = echo_block.shape
    tap_count = filter_matrix.shape[1] // 2
    block_count = bin_count // tap_count
    extended = jnp.concatenate([echo_block, tail_rim], axis=2)
    left_half = extended[:, :, :bin_count].reshape(pulses, planes, block_count, tap_count)
    right_half = extended[:, :, tap_count:].reshape(pulses, planes, block_count, tap_count)
    windows = jnp.concatenate([left_half, right_half], axis=3)
    windows = windows.transpose(0, 2, 1, 3).reshape(pulses * block_count, 2 * planes * tap_count)
    filtered = jnp.dot(windows, filter_matrix, preferred_element_type=jnp.float32)
    filtered = filtered.reshape(pulses, block_count, planes, tap_count).transpose(0, 2, 1, 3)
    return filtered.reshape(pulses, planes, bin_count).astype(jnp.bfloat16)


def cut_windows(block_table, starts):
    block_total = block_table.shape[0]
    first_block = starts // SEG
    second_block = jnp.minimum(first_block + 1, block_total - 1)
    offsets = starts % SEG
    paired = jnp.concatenate([block_table[first_block], block_table[second_block]], axis=3)
    for bit_number in range((SEG - 1).bit_length()):
        step_size = 1 << bit_number
        moved = jnp.concatenate(
            [paired[..., step_size:], jnp.zeros(paired.shape[:-1] + (step_size,), paired.dtype)],
            axis=3,
        )
        chosen = (offsets // step_size % 2 == 1)[:, None, None, None]
        paired = jnp.where(chosen, moved, paired)
    return paired[..., :SEG]


def form_records(block_table, starts, phases, scales):
    windows = cut_windows(block_table, starts)
    cosine = jnp.cos(phases).astype(jnp.bfloat16)
    sine_part = jnp.sin(phases).astype(jnp.bfloat16)
    real_part = windows[:, :, 0]
    imag_part = windows[:, :, 1]
    out_real = jnp.einsum(
        "bk,bks->bs", cosine, real_part, preferred_element_type=jnp.float32
    ) - jnp.einsum("bk,bks->bs", sine_part, imag_part, preferred_element_type=jnp.float32)
    out_imag = jnp.einsum(
        "bk,bks->bs", cosine, imag_part, preferred_element_type=jnp.float32
    ) + jnp.einsum("bk,bks->bs", sine_part, real_part, preferred_element_type=jnp.float32)
    return (jnp.stack([out_real, out_imag], axis=1) * scales[:, None, None]).astype(jnp.bfloat16)


def on_device(
    echo,
    chirp_phase,
    rec_phase,
    rec_start,
    rec_owner,
    rec_row,
    rec_weight,
    rec_count,
    prior,
    interp_weight,
):
    filter_matrix = chirp_matrix(chirp_phase)
    tap_count = chirp_phase.shape[0]
    raw_echo = lax.all_gather(echo, "range", axis=2, tiled=True)
    profiles = compress(raw_echo, jnp.zeros_like(raw_echo[:, :, :tap_count]), filter_matrix)
    pulses, planes, bin_total = profiles.shape
    block_table = profiles.reshape(pulses, planes, bin_total // SEG, SEG).transpose(2, 0, 1, 3)
    slot_count = rec_start.shape[1]
    starts = rec_start[0]
    phases = rec_phase[0]
    owners = rec_owner[0, :, 0]
    dest_rows = rec_row[0]
    weights = rec_weight[0]
    live_mask = (jnp.arange(slot_count) < rec_count[0, 0]).astype(jnp.float32)
    scales = live_mask * weights / jnp.sqrt(jnp.float32(pulses))
    block_size = min(64, slot_count)
    group_count = slot_count // block_size

    def form_group(items):
        return form_records(block_table, items[0], items[1], items[2])

    records = lax.map(
        form_group,
        (
            starts.reshape(group_count, block_size),
            phases.reshape(group_count, block_size, pulses),
            scales.reshape(group_count, block_size),
        ),
    )
    records = records.reshape(slot_count, 2 * SEG)
    pulse_count = lax.axis_size("pulse")
    range_count = lax.axis_size("range")
    owner_total = pulse_count * range_count
    capacity = max(2, 3 * slot_count // (2 * owner_total))
    owner_marks = (owners[:, None] == jnp.arange(owner_total)[None, :]).astype(jnp.int32)
    earlier = jnp.cumsum(owner_marks, axis=0) - owner_marks
    slot_rank = jnp.sum(earlier * owner_marks, axis=1)
    slot_index = owners * capacity + slot_rank
    placement = slot_index[None, :] == jnp.arange(owner_total * capacity)[:, None]
    outgoing = jnp.dot(
        placement.astype(jnp.bfloat16), records, preferred_element_type=jnp.float32
    ).astype(jnp.bfloat16)
    row_slots = jnp.sum(placement.astype(jnp.int32) * dest_rows[None, :], axis=1)
    outgoing = outgoing.reshape(pulse_count, range_count, capacity, 2, SEG)
    row_slots = row_slots.reshape(pulse_count, range_count, capacity)
    incoming, incoming_rows = (
        lax.all_to_all(
            lax.all_to_all(outgoing, "pulse", split_axis=0, concat_axis=0, tiled=True),
            "range",
            split_axis=1,
            concat_axis=1,
            tiled=True,
        ),
        lax.all_to_all(
            lax.all_to_all(row_slots, "pulse", split_axis=0, concat_axis=0, tiled=True),
            "range",
            split_axis=1,
            concat_axis=1,
            tiled=True,
        ),
    )
    incoming = incoming.reshape(-1, 2, SEG)
    incoming_rows = incoming_rows.reshape(-1)
    out_rows = interp_weight.shape[0]
    tile_image = jnp.einsum("rm,mcs->rcs", interp_weight, prior, preferred_element_type=jnp.float32)
    row_table = (incoming_rows[:, None] == jnp.arange(out_rows)[None, :]).astype(jnp.bfloat16)
    tile_image = tile_image + jnp.einsum(
        "jr,jcs->rcs", row_table, incoming, preferred_element_type=jnp.float32
    )
    return tile_image


def solution(mesh):
    placed = (
        P("pulse", None, "range"),
        P(),
        P("range", "pulse", None),
        P("range", "pulse"),
        P("range", "pulse", None),
        P("range", "pulse"),
        P("range", "pulse"),
        P("range", "pulse"),
        P("pulse", None, "range"),
        P(),
    )
    return jax.shard_map(
        on_device, mesh=mesh, in_specs=placed, out_specs=P("pulse", None, "range"), check_vma=False
    )
```

profile of v0, /device:TPU:0, one launch (start us, length us, event | category | flops | bytes accessed | tf_op | source)
XLA Modules:
  0.0 105.9 jit_solution(2789000673935303853)
XLA Ops:
  0.0 0.8 fusion.38
  0.9 0.8 select_reduce_fusion.1
  1.8 0.7 multiply_add_fusion
  2.4 0.8 select_reduce_fusion
  3.2 0.7 reshape.452
  4.0 7.4 %all-to-all-start = ((s32[16,2,6]{2,1,0:T(2,128)}), s32[16,2,6]{2,1,0:T(2,128)S(1)}, u32[]{:S(2)}, u32[]{:S(2)}) async-start(s32[16,2,6]{2,1,0:T(2,128)} %reshape.452), calls=%async_computation | async-start | bytes 32768 | tf_op jit(solution)/shard_map/all_to_all | solution.py:141
  11.3 0.7 sine_multiply_fusion
  12.1 0.5 tile.21
  13.3 0.6 tile.9
  14.1 6.5 %all_gather.3 = bf16[2,2,32768]{2,1,0:T(2,128)(2,1)S(1)} all-gather(bf16[2,2,16384]{2,1,0:T(2,128)(2,1)S(1)} %copy-done.1), channel_id=1, replica_groups=mesh['pulse'=16,'range'=2] {'range'}, dimensions={2}, use_global_device_ids=true | all-gather | bytes 393216 | tf_op jit(solution)/shard_map/all_gather | solution.py:90
  20.8 0.5 maximum_bitcast_fusion
  21.3 0.4 reshape.487
  21.8 0.5 fusion.33
  22.7 0.6 broadcast.1371
  23.3 0.7 reduce.7
  24.8 0.6 broadcast.1370
  25.4 0.6 reduce.6
  26.1 42.6 %while.13 = (s32[]{:T(128)}, bf16[2,64,2,512]{3,2,1,0:T(2,128)(2,1)S(1)}, f32[2,64,2]{1,0,2:T(2,128)S(1)}, s32[2,64]{1,0:T(2,128)S(1)}, bf16[64,2,2,512]{3,2,1,0...) while((s32[]{:T(128)}, bf16[2,64,2,512]{3,2,1,0:T(2,128)(2,1)S(1)}, f32[2,64,2]{1,0,2:T(2,128)S(1)}, ...), condition=%wide.region_4.5_spmd, body=%wide.region_3.4_spmd.sunk | while | flops 3162434 | bytes 28723936 | solution.py:108
  26.3 1.1 %gather_fusion = bf16[64,2,2,512]{3,2,1,0:T(2,128)(2,1)S(1)} fusion(bf16[64,2,2,512]{3,2,1,0:T(2,128)(2,1)S(1)} %get-tuple-element.289, s32[1024]{0:T(1024)S(1)} %get-tuple-element.256), kind=kCustom, calls=%fused_computation.clone.1 | custom fusion | bytes 524544 | tf_op jit(solution)/shard_map/while/body/eval_jaxpr/gather | solution.py:49
  27.6 1.1 %gather_fusion.1 = bf16[64,2,2,512]{3,2,1,0:T(2,128)(2,1)S(1)} fusion(bf16[64,2,2,512]{3,2,1,0:T(2,128)(2,1)S(1)} %get-tuple-element.289, s32[1024]{0:T(1024)S(1)} %get-tuple-element.257), kind=kCustom, calls=%fused_computation.1.clone.1 | custom fusion | bytes 524544 | tf_op jit(solution)/shard_map/while/body/eval_jaxpr/gather | solution.py:49
  28.9 1.0 slice.134
  30.0 1.0 broadcast_select_fusion.18
  31.0 1.0 slice.135
  32.0 1.0 broadcast_select_fusion.19
  33.0 1.0 slice.136
  34.0 1.0 broadcast_select_fusion.20
  35.0 1.0 slice.137
  36.0 1.0 broadcast_select_fusion.21
  37.0 1.0 slice.138
  38.0 1.0 broadcast_select_fusion.22
  39.0 1.0 slice.139
  40.0 1.0 broadcast_select_fusion.23
  41.0 1.0 slice.140
  42.0 1.0 broadcast_select_fusion.24
  43.3 0.7 broadcast_select_fusion.25
  44.3 0.7 broadcast_select_fusion.26
  47.5 1.1 %gather_fusion = bf16[64,2,2,512]{3,2,1,0:T(2,128)(2,1)S(1)} fusion(bf16[64,2,2,512]{3,2,1,0:T(2,128)(2,1)S(1)} %get-tuple-element.289, s32[1024]{0:T(1024)S(1)} %get-tuple-element.256), kind=kCustom, calls=%fused_computation.clone.1 | custom fusion | bytes 524544 | tf_op jit(solution)/shard_map/while/body/eval_jaxpr/gather | solution.py:49
  48.8 1.1 %gather_fusion.1 = bf16[64,2,2,512]{3,2,1,0:T(2,128)(2,1)S(1)} fusion(bf16[64,2,2,512]{3,2,1,0:T(2,128)(2,1)S(1)} %get-tuple-element.289, s32[1024]{0:T(1024)S(1)} %get-tuple-element.257), kind=kCustom, calls=%fused_computation.1.clone.1 | custom fusion | bytes 524544 | tf_op jit(solution)/shard_map/while/body/eval_jaxpr/gather | solution.py:49
  50.2 1.0 slice.134
  51.2 1.0 broadcast_select_fusion.18
  52.2 1.0 slice.135
  53.2 1.0 broadcast_select_fusion.19
  54.2 1.0 slice.136
  55.2 1.0 broadcast_select_fusion.20
  56.2 1.0 slice.137
  57.2 1.0 broadcast_select_fusion.21
  58.2 1.0 slice.138
  59.2 1.0 broadcast_select_fusion.22
  60.2 1.0 slice.139
  61.2 1.0 broadcast_select_fusion.23
  62.2 1.0 slice.140
  63.2 1.0 broadcast_select_fusion.24
  64.5 0.7 broadcast_select_fusion.25
  65.5 0.7 broadcast_select_fusion.26
  69.0 1.0 reshape.458
  70.0 5.9 %all-to-all-start.2 = ((bf16[16,2,6,2,512]{4,3,2,1,0:T(2,128)(2,1)}), bf16[16,2,6,2,512]{4,3,2,1,0:T(2,128)(2,1)S(1)}, u32[]{:S(2)}, u32[]{:S(2)}) async-start(bf16[16,2,6,2,512]{4,3,2,1,0:T(2,128)(2,1)} %reshape.458), calls=%async_computation.2 | async-start | bytes 786432 | tf_op jit(solution)/shard_map/all_to_all | solution.py:134
  75.9 0.7 copy.62
  76.6 11.5 %all-to-all-done.2 = bf16[16,2,6,2,512]{4,3,2,1,0:T(2,128)(2,1)S(1)} async-done(((bf16[16,2,6,2,512]{4,3,2,1,0:T(2,128)(2,1)}), bf16[16,2,6,2,512]{4,3,2,1,0:T(2,128)(2,1)S(1)}, u32[]{:S(2)}, u32[]{:S(2)}) %all-to-all-start.2) | async-done | bytes 393248 | tf_op jit(solution)/shard_map/all_to_all | solution.py:134
  88.1 3.2 %all-to-all-start.1 = ((s32[16,2,6]{0,2,1:T(8,128)}), s32[16,2,6]{0,2,1:T(8,128)S(1)}, u32[]{:S(2)}, u32[]{:S(2)}) async-start(s32[16,2,6]{0,2,1:T(8,128)} %copy.62), calls=%async_computation.1 | async-start | bytes 16384 | tf_op jit(solution)/shard_map/all_to_all | solution.py:140
  91.3 1.0 copy.68
  92.3 2.8 %all-to-all-done.1 = s32[16,2,6]{0,2,1:T(8,128)S(1)} async-done(((s32[16,2,6]{0,2,1:T(8,128)}), s32[16,2,6]{0,2,1:T(8,128)S(1)}, u32[]{:S(2)}, u32[]{:S(2)}) %all-to-all-start.1) | async-done | bytes 800 | tf_op jit(solution)/shard_map/all_to_all | solution.py:140
  95.1 3.5 %all-to-all-start.3 = ((bf16[16,2,6,2,512]{4,3,2,0,1:T(2,128)(2,1)}), bf16[16,2,6,2,512]{4,3,2,0,1:T(2,128)(2,1)S(1)}, u32[]{:S(2)}, u32[]{:S(2)}) async-start(bf16[16,2,6,2,512]{4,3,2,0,1:T(2,128)(2,1)} %copy.68), calls=%async_computation.3 | async-start | bytes 786432 | tf_op jit(solution)/shard_map/all_to_all | solution.py:133
  99.0 5.5 %all-to-all-done.3 = bf16[16,2,6,2,512]{4,3,2,0,1:T(2,128)(2,1)S(1)} async-done(((bf16[16,2,6,2,512]{4,3,2,0,1:T(2,128)(2,1)}), bf16[16,2,6,2,512]{4,3,2,0,1:T(2,128)(2,1)S(1)}, u32[]{:S(2)}, u32[]{:S(2)}) %all-to-all-start.3) | async-done | bytes 393248 | tf_op jit(solution)/shard_map/all_to_all | solution.py:133
  105.0 0.9 copy.71
  (95 shorter events, 10.2 us)
Async XLA Ops:
  0.0 98.6 %copy-start = (bf16[32,2,512]{2,1,0:T(2,128)(2,1)S(1)}, bf16[32,2,512]{2,1,0:T(2,128)(2,1)}, u32[]{:S(2)}) copy-start(bf16[32,2,512]{2,1,0:T(2,128)(2,1)} %param.20) | copy-start | bytes 196612
  4.0 66.1 %all-to-all-start = ((s32[16,2,6]{2,1,0:T(2,128)}), s32[16,2,6]{2,1,0:T(2,128)S(1)}, u32[]{:S(2)}, u32[]{:S(2)}) async-start(s32[16,2,6]{2,1,0:T(2,128)} %reshape.452), calls=%async_computation | async-start | bytes 32768 | tf_op jit(solution)/shard_map/all_to_all | solution.py:141
  12.1 0.7 copy-start.4
  13.2 0.9 copy-start.1
  21.8 1.5 %copy-start.5 = (f32[1,128]{1,0:T(1,128)S(1)}, f32[1,128]{1,0:T(1,128)}, u32[]{:S(2)}) copy-start(f32[1,128]{1,0:T(1,128)} %param.18) | copy-start | bytes 1540
  21.8 3.0 %copy-start.3 = (f32[1,128,2]{1,2,0:T(2,128)S(1)}, f32[1,128,2]{1,2,0:T(2,128)}, u32[]{:S(2)}) copy-start(f32[1,128,2]{1,2,0:T(2,128)} %param.14) | copy-start | bytes 3076
  21.8 3.6 %copy-start.6 = (s32[1,128]{1,0:T(1,128)S(1)}, s32[1,128]{1,0:T(1,128)}, u32[]{:S(2)}) copy-start(s32[1,128]{1,0:T(1,128)} %param.15) | copy-start | bytes 1540
  70.0 28.5 %copy-start.2 = (bf16[64,32]{0,1:T(8,128)(2,1)S(1)}, bf16[64,32]{0,1:T(8,128)(2,1)}, u32[]{:S(2)}) copy-start(bf16[64,32]{0,1:T(8,128)(2,1)} %param.21) | copy-start | bytes 12292
  70.0 18.0 %all-to-all-start.2 = ((bf16[16,2,6,2,512]{4,3,2,1,0:T(2,128)(2,1)}), bf16[16,2,6,2,512]{4,3,2,1,0:T(2,128)(2,1)S(1)}, u32[]{:S(2)}, u32[]{:S(2)}) async-start(bf16[16,2,6,2,512]{4,3,2,1,0:T(2,128)(2,1)} %reshape.458), calls=%async_computation.2 | async-start | bytes 786432 | tf_op jit(solution)/shard_map/all_to_all | solution.py:134
  88.1 7.0 %all-to-all-start.1 = ((s32[16,2,6]{0,2,1:T(8,128)}), s32[16,2,6]{0,2,1:T(8,128)S(1)}, u32[]{:S(2)}, u32[]{:S(2)}) async-start(s32[16,2,6]{0,2,1:T(8,128)} %copy.62), calls=%async_computation.1 | async-start | bytes 16384 | tf_op jit(solution)/shard_map/all_to_all | solution.py:140
  95.1 9.4 %all-to-all-start.3 = ((bf16[16,2,6,2,512]{4,3,2,0,1:T(2,128)(2,1)}), bf16[16,2,6,2,512]{4,3,2,0,1:T(2,128)(2,1)S(1)}, u32[]{:S(2)}, u32[]{:S(2)}) async-start(bf16[16,2,6,2,512]{4,3,2,0,1:T(2,128)(2,1)} %copy.68), calls=%async_computation.3 | async-start | bytes 786432 | tf_op jit(solution)/shard_map/all_to_all | solution.py:133
where the time goes:
time: 106 us
  local copies, waits for them, and re-layouts  31.5 us (30%)
  other arithmetic  23.3 us (22%)
  starting transfers between devices  19.9 us (19%)
  waiting for transfers between devices  19.8 us (19%)
  blocking collectives  6.46 us (6%)
  matrix products  3.38 us (3%)
    select_n x18, other arithmetic, cut_windows(): paired = jnp.where(chosen, moved, paired)  16.4 us
    slice x18, local copies, waits for them, and re-layouts, cut_windows(): paired[..., step_size:]  15.4 us
    all_to_all x1, waiting for transfers between devices, on_device(): lax.all_to_all(outgoing, 'pulse', split_axis=0, concat_axis=0, tiled=True)  11.5 us
    all_to_all x1, starting transfers between devices, on_device(): lax.all_to_all(row_slots, 'pulse', split_axis=0, concat_axis=0, tiled=True)  7.39 us
    all_gather x1, blocking collectives, on_device(): raw_echo = lax.all_gather(echo, 'range', axis=2, tiled=True)  6.46 us
    all_to_all x1, starting transfers between devices, on_device(): lax.all_to_all(outgoing, 'pulse', split_axis=0, concat_axis=0, tiled=True)  5.85 us
    all_to_all x1, waiting for transfers between devices, on_device(): lax.all_to_all(lax.all_to_all(outgoing, 'pulse', split_axis=0, concat_axi...  5.52 us
    all_to_all x1, starting transfers between devices, on_device(): lax.all_to_all(lax.all_to_all(outgoing, 'pulse', split_axis=0, concat_axi...  3.47 us
  transfers between devices with their start and end apart: 4, of which 3 were waited for; matrix products, arithmetic and copies ran while one was open for 50% of the time, Pallas kernels for 0%

commit v1 on v0

--- a/solution.py
+++ b/solution.py
@@ -4,6 +4,18 @@
 from jax.sharding import PartitionSpec as P
 
 SEG = 512
+
+
+def doubled_up(x, axis, dim):
+    ways, here = (lax.axis_size(axis), lax.axis_index(axis))
+    grown, reach = (x, 1)
+    while reach < ways:
+        theirs = lax.ppermute(grown, axis, [(d, d ^ reach) for d in range(ways)])
+        mine_first = jnp.concatenate([grown, theirs], axis=dim)
+        theirs_first = jnp.concatenate([theirs, grown], axis=dim)
+        grown = jnp.where(here & reach == 0, mine_first, theirs_first)
+        reach = 2 * reach
+    return grown
 
 
 def chirp_matrix(chirp_phase):
@@ -87,7 +99,7 @@
 ):
     filter_matrix = chirp_matrix(chirp_phase)
     tap_count = chirp_phase.shape[0]
-    raw_echo = lax.all_gather(echo, "range", axis=2, tiled=True)
+    raw_echo = doubled_up(echo, "range", 2)
     profiles = compress(raw_echo, jnp.zeros_like(raw_echo[:, :, :tap_count]), filter_matrix)
     pulses, planes, bin_total = profiles.shape
     block_table = profiles.reshape(pulses, planes, bin_total // SEG, SEG).transpose(2, 0, 1, 3)

time: 106 us -> 103 us (0.972)
  blocking collectives: 6.46 us -> 0 us
  starting transfers between devices: 19.9 us -> 21.7 us
    all_gather x1 -> x0, blocking collectives: 6.46 us -> none  [on_device(): raw_echo = lax.all_gather(echo, 'range', axis=2, tiled=True)]
    ppermute x0 -> x1, starting transfers between devices: none -> 3 us  [doubled_up(): theirs = lax.ppermute(grown, axis, [(d, d ^ reach) for d in range(ways)])]
    all_to_all x1, starting transfers between devices: 7.39 us -> 5.91 us  [on_device(): lax.all_to_all(row_slots, 'pulse', split_axis=0, concat_axis=0, tiled=True)]
  transfers between devices with their start and end apart: 4 -> 5, of which waited for: 3 -> 3; matrix products, arithmetic and copies ran while one was open for 50% -> 56% of each run, Pallas kernels for 0% -> 0%
where the time goes in v1:
time: 103 us; the launch traced here: 102 us
  local copies, waits for them, and re-layouts  31.4 us (30%)
  other arithmetic  24.3 us (24%)
  starting transfers between devices  21.7 us (21%)
  waiting for transfers between devices  19.8 us (19%)
  matrix products  3.33 us (3%)
    select_n x18, other arithmetic, cut_windows(): paired = jnp.where(chosen, moved, paired)  16.4 us
    slice x18, local copies, waits for them, and re-layouts, cut_windows(): paired[..., step_size:]  15.4 us
    all_to_all x1, waiting for transfers between devices, on_device(): lax.all_to_all(outgoing, 'pulse', split_axis=0, concat_axis=0, tiled=True)  11.5 us
    all_to_all x1, starting transfers between devices, on_device(): lax.all_to_all(outgoing, 'pulse', split_axis=0, concat_axis=0, tiled=True)  6.14 us
    all_to_all x1, starting transfers between devices, on_device(): lax.all_to_all(row_slots, 'pulse', split_axis=0, concat_axis=0, tiled=True)  5.91 us
    all_to_all x1, waiting for transfers between devices, on_device(): lax.all_to_all(lax.all_to_all(outgoing, 'pulse', split_axis=0, concat_axi...  5.52 us
    all_to_all x1, starting transfers between devices, on_device(): lax.all_to_all(lax.all_to_all(outgoing, 'pulse', split_axis=0, concat_axi...  3.47 us
    all_to_all x1, starting transfers between devices, on_device(): lax.all_to_all(lax.all_to_all(row_slots, 'pulse', split_axis=0, concat_ax...  3.23 us
  transfers between devices with their start and end apart: 5, of which 3 were waited for; matrix products, arithmetic and copies ran while one was open for 56% of the time, Pallas kernels for 0%

profile of v1, /device:TPU:0, one launch (start us, length us, event | category | flops | bytes accessed | tf_op | source)
XLA Modules:
  0.0 102.2 jit_solution(2727626767383465408)
XLA Ops:
  0.0 3.0 %collective-permute-start = (bf16[2,2,16384]{2,1,0:T(2,128)(2,1)}, bf16[2,2,16384]{2,1,0:T(2,128)(2,1)S(1)}, u32[]{:S(2)}, u32[]{:S(2)}) collective-permute-start(bf16[2,2,16384]{2,1,0:T(2,128)(2,1)} %param.12), channel_id=1, source_target_pairs={{0,1},{1,0},{2,3},{3,2},{4,5},{5,4},{6,7},{7,6},{8,9},{9,8},{10,11... | collective-permute-start | bytes 393224 | tf_op jit(solution)/shard_map/ppermute | solution.py:13
  3.0 0.7 fusion.38
  3.9 0.8 select_reduce_fusion.1
  4.7 0.7 multiply_add_fusion
  5.4 0.8 select_reduce_fusion
  6.2 0.7 reshape.454
  6.9 5.9 %all-to-all-start = ((s32[16,2,6]{2,1,0:T(2,128)}), s32[16,2,6]{2,1,0:T(2,128)S(1)}, u32[]{:S(2)}, u32[]{:S(2)}) async-start(s32[16,2,6]{2,1,0:T(2,128)} %reshape.454), calls=%async_computation | async-start | bytes 32768 | tf_op jit(solution)/shard_map/all_to_all | solution.py:153
  12.8 0.7 sine_multiply_fusion
  13.6 0.5 tile.21
  14.8 0.6 tile.9
  15.6 0.6 broadcast.1372
  16.2 0.6 reduce.7
  17.6 0.5 broadcast.1371
  18.2 0.7 reduce.6
  19.7 0.6 broadcast_select_fusion.10
  20.3 0.5 maximum_bitcast_fusion
  21.2 0.5 fusion.33
  22.0 42.6 %while.13 = (s32[]{:T(128)}, bf16[2,64,2,512]{3,2,1,0:T(2,128)(2,1)S(1)}, f32[2,64,2]{1,0,2:T(2,128)S(1)}, s32[2,64]{1,0:T(2,128)S(1)}, bf16[64,2,2,512]{3,2,1,0...) while((s32[]{:T(128)}, bf16[2,64,2,512]{3,2,1,0:T(2,128)(2,1)S(1)}, f32[2,64,2]{1,0,2:T(2,128)S(1)}, ...), condition=%wide.region_4.5_spmd, body=%wide.region_3.4_spmd.sunk | while | flops 3162434 | bytes 28723936 | solution.py:120
  22.3 1.1 %gather_fusion = bf16[64,2,2,512]{3,2,1,0:T(2,128)(2,1)S(1)} fusion(bf16[64,2,2,512]{3,2,1,0:T(2,128)(2,1)S(1)} %get-tuple-element.289, s32[1024]{0:T(1024)S(1)} %get-tuple-element.256), kind=kCustom, calls=%fused_computation.clone.1 | custom fusion | bytes 524544 | tf_op jit(solution)/shard_map/while/body/eval_jaxpr/gather | solution.py:61
  23.6 1.1 %gather_fusion.1 = bf16[64,2,2,512]{3,2,1,0:T(2,128)(2,1)S(1)} fusion(bf16[64,2,2,512]{3,2,1,0:T(2,128)(2,1)S(1)} %get-tuple-element.289, s32[1024]{0:T(1024)S(1)} %get-tuple-element.257), kind=kCustom, calls=%fused_computation.1.clone.1 | custom fusion | bytes 524544 | tf_op jit(solution)/shard_map/while/body/eval_jaxpr/gather | solution.py:61
  24.9 1.0 slice.134
  26.0 1.0 broadcast_select_fusion.20
  26.9 1.0 slice.135
  27.9 1.0 broadcast_select_fusion.21
  28.9 1.0 slice.136
  29.9 1.0 broadcast_select_fusion.22
  30.9 1.0 slice.137
  31.9 1.0 broadcast_select_fusion.23
  32.9 1.0 slice.138
  33.9 1.0 broadcast_select_fusion.24
  34.9 1.0 slice.139
  36.0 1.0 broadcast_select_fusion.25
  36.9 1.0 slice.140
  38.0 1.0 broadcast_select_fusion.26
  39.3 0.7 broadcast_select_fusion.27
  40.2 0.7 broadcast_select_fusion.28
  43.5 1.1 %gather_fusion = bf16[64,2,2,512]{3,2,1,0:T(2,128)(2,1)S(1)} fusion(bf16[64,2,2,512]{3,2,1,0:T(2,128)(2,1)S(1)} %get-tuple-element.289, s32[1024]{0:T(1024)S(1)} %get-tuple-element.256), kind=kCustom, calls=%fused_computation.clone.1 | custom fusion | bytes 524544 | tf_op jit(solution)/shard_map/while/body/eval_jaxpr/gather | solution.py:61
  44.8 1.1 %gather_fusion.1 = bf16[64,2,2,512]{3,2,1,0:T(2,128)(2,1)S(1)} fusion(bf16[64,2,2,512]{3,2,1,0:T(2,128)(2,1)S(1)} %get-tuple-element.289, s32[1024]{0:T(1024)S(1)} %get-tuple-element.257), kind=kCustom, calls=%fused_computation.1.clone.1 | custom fusion | bytes 524544 | tf_op jit(solution)/shard_map/while/body/eval_jaxpr/gather | solution.py:61
  46.1 1.0 slice.134
  47.2 1.0 broadcast_select_fusion.20
  48.2 1.0 slice.135
  49.2 1.0 broadcast_select_fusion.21
  50.2 1.0 slice.136
  51.2 1.0 broadcast_select_fusion.22
  52.2 1.0 slice.137
  53.2 1.0 broadcast_select_fusion.23
  54.2 1.0 slice.138
  55.2 1.0 broadcast_select_fusion.24
  56.2 1.0 slice.139
  57.2 1.0 broadcast_select_fusion.25
  58.2 1.0 slice.140
  59.2 1.0 broadcast_select_fusion.26
  60.5 0.7 broadcast_select_fusion.27
  61.5 0.7 broadcast_select_fusion.28
  65.0 1.0 reshape.459
  66.0 6.1 %all-to-all-start.2 = ((bf16[16,2,6,2,512]{4,3,2,1,0:T(2,128)(2,1)}), bf16[16,2,6,2,512]{4,3,2,1,0:T(2,128)(2,1)S(1)}, u32[]{:S(2)}, u32[]{:S(2)}) async-start(bf16[16,2,6,2,512]{4,3,2,1,0:T(2,128)(2,1)} %reshape.459), calls=%async_computation.2 | async-start | bytes 786432 | tf_op jit(solution)/shard_map/all_to_all | solution.py:146
  72.1 0.7 copy.77
  72.8 11.5 %all-to-all-done.2 = bf16[16,2,6,2,512]{4,3,2,1,0:T(2,128)(2,1)S(1)} async-done(((bf16[16,2,6,2,512]{4,3,2,1,0:T(2,128)(2,1)}), bf16[16,2,6,2,512]{4,3,2,1,0:T(2,128)(2,1)S(1)}, u32[]{:S(2)}, u32[]{:S(2)}) %all-to-all-start.2) | async-done | bytes 393248 | tf_op jit(solution)/shard_map/all_to_all | solution.py:146
  84.3 3.2 %all-to-all-start.1 = ((s32[16,2,6]{0,2,1:T(8,128)}), s32[16,2,6]{0,2,1:T(8,128)S(1)}, u32[]{:S(2)}, u32[]{:S(2)}) async-start(s32[16,2,6]{0,2,1:T(8,128)} %copy.77), calls=%async_computation.1 | async-start | bytes 16384 | tf_op jit(solution)/shard_map/all_to_all | solution.py:152
  87.5 1.0 copy.86
  88.6 2.8 %all-to-all-done.1 = s32[16,2,6]{0,2,1:T(8,128)S(1)} async-done(((s32[16,2,6]{0,2,1:T(8,128)}), s32[16,2,6]{0,2,1:T(8,128)S(1)}, u32[]{:S(2)}, u32[]{:S(2)}) %all-to-all-start.1) | async-done | bytes 800 | tf_op jit(solution)/shard_map/all_to_all | solution.py:152
  91.3 3.5 %all-to-all-start.3 = ((bf16[16,2,6,2,512]{4,3,2,0,1:T(2,128)(2,1)}), bf16[16,2,6,2,512]{4,3,2,0,1:T(2,128)(2,1)S(1)}, u32[]{:S(2)}, u32[]{:S(2)}) async-start(bf16[16,2,6,2,512]{4,3,2,0,1:T(2,128)(2,1)} %copy.86), calls=%async_computation.3 | async-start | bytes 786432 | tf_op jit(solution)/shard_map/all_to_all | solution.py:145
  95.3 5.5 %all-to-all-done.3 = bf16[16,2,6,2,512]{4,3,2,0,1:T(2,128)(2,1)S(1)} async-done(((bf16[16,2,6,2,512]{4,3,2,0,1:T(2,128)(2,1)}), bf16[16,2,6,2,512]{4,3,2,0,1:T(2,128)(2,1)S(1)}, u32[]{:S(2)}, u32[]{:S(2)}) %all-to-all-start.3) | async-done | bytes 393248 | tf_op jit(solution)/shard_map/all_to_all | solution.py:145
  101.3 0.9 copy.89
  (98 shorter events, 10.9 us)
Async XLA Ops:
  0.0 94.8 %copy-start = (bf16[32,2,512]{2,1,0:T(2,128)(2,1)S(1)}, bf16[32,2,512]{2,1,0:T(2,128)(2,1)}, u32[]{:S(2)}) copy-start(bf16[32,2,512]{2,1,0:T(2,128)(2,1)} %param.20) | copy-start | bytes 196612
  0.0 19.1 %collective-permute-start = (bf16[2,2,16384]{2,1,0:T(2,128)(2,1)}, bf16[2,2,16384]{2,1,0:T(2,128)(2,1)S(1)}, u32[]{:S(2)}, u32[]{:S(2)}) collective-permute-start(bf16[2,2,16384]{2,1,0:T(2,128)(2,1)} %param.12), channel_id=1, source_target_pairs={{0,1},{1,0},{2,3},{3,2},{4,5},{5,4},{6,7},{7,6},{8,9},{9,8},{10,11... | collective-permute-start | bytes 393224 | tf_op jit(solution)/shard_map/ppermute | solution.py:13
  6.9 59.1 %all-to-all-start = ((s32[16,2,6]{2,1,0:T(2,128)}), s32[16,2,6]{2,1,0:T(2,128)S(1)}, u32[]{:S(2)}, u32[]{:S(2)}) async-start(s32[16,2,6]{2,1,0:T(2,128)} %reshape.454), calls=%async_computation | async-start | bytes 32768 | tf_op jit(solution)/shard_map/all_to_all | solution.py:153
  13.6 0.7 copy-start.4
  14.7 1.5 %copy-start.5 = (f32[1,128]{1,0:T(1,128)S(1)}, f32[1,128]{1,0:T(1,128)}, u32[]{:S(2)}) copy-start(f32[1,128]{1,0:T(1,128)} %param.18) | copy-start | bytes 1540
  14.7 2.8 %copy-start.3 = (f32[1,128,2]{1,2,0:T(2,128)S(1)}, f32[1,128,2]{1,2,0:T(2,128)}, u32[]{:S(2)}) copy-start(f32[1,128,2]{1,2,0:T(2,128)} %param.14) | copy-start | bytes 3076
  14.7 3.5 %copy-start.6 = (s32[1,128]{1,0:T(1,128)S(1)}, s32[1,128]{1,0:T(1,128)}, u32[]{:S(2)}) copy-start(s32[1,128]{1,0:T(1,128)} %param.15) | copy-start | bytes 1540
  15.6 3.5 %copy-start.1 = (bf16[2,2,16384]{2,1,0:T(2,128)(2,1)S(1)}, bf16[2,2,16384]{2,1,0:T(2,128)(2,1)}, u32[]{:S(2)}) copy-start(bf16[2,2,16384]{2,1,0:T(2,128)(2,1)} %param.12) | copy-start | bytes 393220
  66.0 28.8 %copy-start.2 = (bf16[64,32]{0,1:T(8,128)(2,1)S(1)}, bf16[64,32]{0,1:T(8,128)(2,1)}, u32[]{:S(2)}) copy-start(bf16[64,32]{0,1:T(8,128)(2,1)} %param.21) | copy-start | bytes 12292
  66.0 18.3 %all-to-all-start.2 = ((bf16[16,2,6,2,512]{4,3,2,1,0:T(2,128)(2,1)}), bf16[16,2,6,2,512]{4,3,2,1,0:T(2,128)(2,1)S(1)}, u32[]{:S(2)}, u32[]{:S(2)}) async-start(bf16[16,2,6,2,512]{4,3,2,1,0:T(2,128)(2,1)} %reshape.459), calls=%async_computation.2 | async-start | bytes 786432 | tf_op jit(solution)/shard_map/all_to_all | solution.py:146
  84.3 7.0 %all-to-all-start.1 = ((s32[16,2,6]{0,2,1:T(8,128)}), s32[16,2,6]{0,2,1:T(8,128)S(1)}, u32[]{:S(2)}, u32[]{:S(2)}) async-start(s32[16,2,6]{0,2,1:T(8,128)} %copy.77), calls=%async_computation.1 | async-start | bytes 16384 | tf_op jit(solution)/shard_map/all_to_all | solution.py:152
  91.3 9.4 %all-to-all-start.3 = ((bf16[16,2,6,2,512]{4,3,2,0,1:T(2,128)(2,1)}), bf16[16,2,6,2,512]{4,3,2,0,1:T(2,128)(2,1)S(1)}, u32[]{:S(2)}, u32[]{:S(2)}) async-start(bf16[16,2,6,2,512]{4,3,2,0,1:T(2,128)(2,1)} %copy.86), calls=%async_computation.3 | async-start | bytes 786432 | tf_op jit(solution)/shard_map/all_to_all | solution.py:145
